TPU v7x, 256 devices: a whole 4x4x8 slice. The times are simulated.
256 devices in a mesh: dp: 64 (over y_hi, z, x), mp: 4 (over y_lo, core).
Axes of the slice: x: 4, y: 4 (y_hi: 2, y_lo: 2; y = y_hi * 2 + y_lo), z: 8, core: 2. Of those that a mesh axis runs over, the one named last changes fastest.
Arguments:
- image_feats: bfloat16 [65536, 1152], P('dp'), may hold values from -16 to 16
- text_feats: bfloat16 [65536, 1152], P('dp'), may hold values from -16 to 16
- image_head: bfloat16 [1152, 1152], P(None, 'mp')
- text_head: bfloat16 [1152, 1152], P(None, 'mp')
- hard_tiles: int32 [512, 16], P('dp'), may hold values from 0 to 511, as said below
- logit_scale: float32 [1], replicated, may hold values from 6 to 16
- logit_bias: float32 [1], replicated, may hold values from -4 to -1
Outputs:
- head_grad_img: float32 [1152, 1152], P('dp', 'mp')
- head_grad_txt: float32 [1152, 1152], P('dp', 'mp')
Inputs may be any that keep to these rules, and one draw needn't show every extreme that they name: `hard_tiles`: row tile g lies in block i = g // 8; with o running over -2 .. -1, 1 .. 2 in order as o_0 .. o_(3), entries 4 * k to 4 * k + 3 of row g are 4 different tiles of block (i + o_k) mod 64, and block j holds tiles 8 * j to 8 * j + 7.
All inputs are finite; a program needn't handle non-finite values.
Results may differ from a plain program's by a relative error of at most 0.0015.
Values may be sent and summed in bfloat16 or wider, within the bound.
No kernel may reach another device: no remote copies, remote signals or barrier semaphores. Data moves between devices by JAX's collectives and lax.ppermute only.
A program may use at most 128 MiB of HBM per device.

v0:
```python
import jax
import jax.numpy as jnp
from jax import lax
from jax.sharding import PartitionSpec as P

EPSILON = 1e-06


def shifted(value, axis, steps):
    count = lax.axis_size(axis)
    pairs = [(source, (source + steps) % count) for source in range(count)]
    return lax.ppermute(value, axis, pairs)


def shards(image_feats, text_feats, image_head, text_head, hard_tiles, logit_scale, logit_bias):
    row_count = image_feats.shape[0]
    width_part = image_head.shape[1]
    per_block = row_count // 128
    model_count = lax.axis_size("mp")
    model_index = lax.axis_index("mp")
    tiles_share = per_block // model_count
    span_blocks = min(2, (lax.axis_size("dp") - 1) // 2)
    pick_count = hard_tiles.shape[1] // (2 * span_blocks)
    temp_scale = logit_scale[0]
    shift_bias = logit_bias[0]
    image_proj = jnp.dot(image_feats, image_head, preferred_element_type=jnp.float32)
    text_proj = jnp.dot(text_feats, text_head, preferred_element_type=jnp.float32)
    norm_img, norm_txt = lax.psum(
        (jnp.sum(image_proj * image_proj, axis=1), jnp.sum(text_proj * text_proj, axis=1)), "mp"
    )
    inverse_img = lax.rsqrt(norm_img + EPSILON)
    inverse_txt = lax.rsqrt(norm_txt + EPSILON)
    image_unit = (image_proj * inverse_img[:, None]).astype(jnp.bfloat16)
    text_unit = (text_proj * inverse_txt[:, None]).astype(jnp.bfloat16)
    image_tiles = image_unit.reshape(per_block, 128, width_part)
    local_ids = hard_tiles % per_block
    image_mine = lax.all_to_all(image_unit, "mp", split_axis=0, concat_axis=1, tiled=True)
    mine_tiles = image_mine.reshape(tiles_share, 128, image_mine.shape[1])
    text_full = lax.all_gather(text_unit, "mp", axis=1, tiled=True)
    partial_value = jnp.dot(image_unit, text_unit.T, preferred_element_type=jnp.float32)
    scores = lax.psum(partial_value, "mp")
    diagonal_mask = jnp.eye(row_count, dtype=jnp.float32)
    weight = (
        temp_scale * (jax.nn.sigmoid(temp_scale * scores + shift_bias) - diagonal_mask)
    ).astype(jnp.bfloat16)
    grad_img = jnp.dot(weight, text_unit, preferred_element_type=jnp.float32)
    grad_txt = jnp.einsum("pq,pe->qe", weight, image_unit, preferred_element_type=jnp.float32)
    current = shifted(text_full, "dp", -span_blocks)
    carried = jnp.zeros_like(text_proj)
    for step_index in range(2 * span_blocks + 1):
        if step_index > 0:
            current = shifted(current, "dp", 1)
            carried = shifted(carried, "dp", 1)
        offset = span_blocks - step_index
        if offset != 0:
            slot_index = offset + span_blocks if offset < 0 else offset + span_blocks - 1
            picked = local_ids[:, pick_count * slot_index : pick_count * slot_index + pick_count]
            picked_mine = lax.dynamic_slice_in_dim(
                picked, model_index * tiles_share, tiles_share, 0
            )
            wide_tiles = current.reshape(per_block, 128, current.shape[1])
            chosen_wide = jnp.take(wide_tiles, picked_mine, axis=0)
            pair_part = jnp.einsum(
                "rpe,rkqe->rkpq", mine_tiles, chosen_wide, preferred_element_type=jnp.float32
            )
            weight_part = (temp_scale * jax.nn.sigmoid(temp_scale * pair_part + shift_bias)).astype(
                jnp.bfloat16
            )
            pair_weight = lax.all_gather(weight_part, "mp", axis=0, tiled=True)
            text_local = lax.dynamic_slice_in_dim(current, model_index * width_part, width_part, 1)
            chosen = jnp.take(text_local.reshape(per_block, 128, width_part), picked, axis=0)
            into_img = jnp.einsum(
                "rkpq,rkqe->rpe", pair_weight, chosen, preferred_element_type=jnp.float32
            )
            into_sel = jnp.einsum(
                "rkpq,rpe->rkqe", pair_weight, image_tiles, preferred_element_type=jnp.float32
            )
            onehot = (
                picked[:, :, None] == jnp.arange(per_block, dtype=jnp.int32)[None, None, :]
            ).astype(jnp.float32)
            into_txt = jnp.einsum(
                "rkt,rkqe->tqe", onehot, into_sel, precision=lax.Precision.HIGHEST
            )
            into_img, into_txt = (
                into_img.reshape(row_count, width_part),
                into_txt.reshape(row_count, width_part),
            )
            grad_img = grad_img + into_img
            carried = carried + into_txt
    grad_txt = grad_txt + shifted(carried, "dp", -span_blocks)
    dots_img, dots_txt = lax.psum(
        (jnp.sum(image_proj * grad_img, axis=1), jnp.sum(text_proj * grad_txt, axis=1)), "mp"
    )
    cube_img = dots_img * inverse_img * inverse_img * inverse_img
    cube_txt = dots_txt * inverse_txt * inverse_txt * inverse_txt
    dproj_img = (inverse_img[:, None] * grad_img - cube_img[:, None] * image_proj).astype(
        jnp.bfloat16
    )
    dproj_txt = (inverse_txt[:, None] * grad_txt - cube_txt[:, None] * text_proj).astype(
        jnp.bfloat16
    )
    local_img = jnp.einsum("nd,ne->de", image_feats, dproj_img, preferred_element_type=jnp.float32)
    local_txt = jnp.einsum("nd,ne->de", text_feats, dproj_txt, preferred_element_type=jnp.float32)
    head_grad_img, head_grad_txt = (
        lax.psum_scatter(local_img, "dp", scatter_dimension=0, tiled=True),
        lax.psum_scatter(local_txt, "dp", scatter_dimension=0, tiled=True),
    )
    return (head_grad_img, head_grad_txt)


def solution(mesh):
    placed = (P("dp", None), P("dp", None), P(None, "mp"), P(None, "mp"), P("dp", None), P(), P())
    return jax.shard_map(
        shards,
        mesh=mesh,
        in_specs=placed,
        out_specs=(P("dp", "mp"), P("dp", "mp")),
        check_vma=False,
    )
```

profile of v0, /device:TPU:2, one launch (start us, length us, event | category | flops | bytes accessed | tf_op | source)
XLA Modules:
  0.0 1373.6 jit_solution(13354665672646321138)
XLA Ops:
  8.8 3.2 multiply_reduce_fusion.3
  13.0 7.1 all-reduce.4
  21.2 36.2 %all-gather.6.cloned.1.call-done = bf16[1024,1152]{0,1:T(8,128)(2,1)} async-done(((bf16[1024,288]{0,1:T(8,128)(2,1)}), bf16[1024,1152]{0,1:T(8,128)(2,1)}) %all-gather.6.cloned.1.call-update) | async-done | bytes 2359312 | tf_op jit(solution)/shard_map/all_gather | solution.py:39
  57.4 7.0 collective-permute-start
  64.4 51.6 %collective-permute-done = bf16[1024,1152]{0,1:T(8,128)(2,1)} collective-permute-done((bf16[1024,1152]{0,1:T(8,128)(2,1)}, bf16[1024,1152]{0,1:T(8,128)(2,1)}, u32[]{:S(2)}, u32[]{:S(2)}) %collective-permute-start) | collective-permute-done | bytes 2359328 | tf_op jit(solution)/shard_map/ppermute | solution.py:12
  119.1 4.2 all-to-all-start
  129.1 3.8 all-to-all-done
  132.9 2.5 reshape.81
  135.4 2.9 copy.125
  138.3 4.3 copy.141
  142.7 4.0 gather_fusion
  146.7 3.3 fusion.160
  154.4 14.8 %collective-permute-done.1 = bf16[1024,1152]{0,1:T(8,128)(2,1)} collective-permute-done((bf16[1024,1152]{0,1:T(8,128)(2,1)}, bf16[1024,1152]{0,1:T(8,128)(2,1)}, u32[]{:S(2)}, u32[]{:S(2)}) %collective-permute-start.1) | collective-permute-done | bytes 2359328 | tf_op jit(solution)/shard_map/ppermute | solution.py:12
  170.8 4.3 copy.144
  175.1 4.0 gather_fusion.2
  179.1 3.3 fusion.148
  182.5 1.8 copy.98
  184.3 4.5 fusion.197
  188.9 65.8 %collective-permute-done.2 = bf16[1024,1152]{0,1:T(8,128)(2,1)} collective-permute-done((bf16[1024,1152]{0,1:T(8,128)(2,1)}, bf16[1024,1152]{0,1:T(8,128)(2,1)}, u32[]{:S(2)}, u32[]{:S(2)}) %collective-permute-start.2) | collective-permute-done | bytes 2359328 | tf_op jit(solution)/shard_map/ppermute | solution.py:12
  275.2 2.2 fusion.168
  277.4 6.1 fusion.6
  286.6 28.2 %collective-permute-done.3 = bf16[1024,1152]{0,1:T(8,128)(2,1)} collective-permute-done((bf16[1024,1152]{0,1:T(8,128)(2,1)}, bf16[1024,1152]{0,1:T(8,128)(2,1)}, u32[]{:S(2)}, u32[]{:S(2)}) %collective-permute-start.3) | collective-permute-done | bytes 2359328 | tf_op jit(solution)/shard_map/ppermute | solution.py:12
  315.1 2.2 fusion.170
  317.2 6.1 fusion.4
  323.4 16.7 %collective-permute-done.5 = f32[1024,288]{0,1:T(8,128)} collective-permute-done((f32[1024,288]{0,1:T(8,128)}, f32[1024,288]{0,1:T(8,128)}, u32[]{:S(2)}, u32[]{:S(2)}) %collective-permute-start.5) | collective-permute-done | bytes 1179680 | tf_op jit(solution)/shard_map/ppermute | solution.py:12
  340.1 2.7 bitcast_add_fusion.2
  342.8 4.3 copy.147
  347.1 4.0 gather_fusion.4
  351.1 3.3 fusion.136
  354.4 1.8 copy.103
  356.2 157.7 %all-reduce.8.cloned.1.call-done = f32[1024,1024]{1,0:T(8,128)} async-done(((f32[1024,1024]{1,0:T(8,128)}), f32[1024,1024]{1,0:T(8,128)}) %all-reduce.8.cloned.1.call-update) | async-done | bytes 4194320 | tf_op jit(solution)/shard_map/psum | solution.py:41
  513.9 4.7 multiply_convert_fusion
  518.6 2.0 copy_bitcast_fusion.4
  520.6 3.4 gather_fusion.1
  524.0 3.8 fusion.32
  527.9 1.9 collective-permute-start.7
  529.7 4.3 copy.150
  534.0 4.1 gather_fusion.6
  538.2 3.3 fusion.124
  541.5 1.8 copy.108
  543.4 2.0 copy_bitcast_fusion.3
  545.4 3.3 gather_fusion.3
  548.7 2.2 fusion.172
  550.9 6.1 fusion.2
  557.0 2.8 bitcast_add_fusion.1
  561.3 1.9 fusion.35
  563.2 2.0 copy_bitcast_fusion.2
  565.2 3.3 gather_fusion.5
  568.5 14.4 %all-gather.14.cloned.1.call-done = bf16[8,4,128,128]{3,2,1,0:T(8,128)(2,1)} async-done(((bf16[2,4,128,128]{3,2,1,0:T(8,128)(2,1)}), bf16[8,4,128,128]{3,2,1,0:T(8,128)(2,1)}) %all-gather.14.cloned.1.call-update) | async-done | bytes 1048592 | tf_op jit(solution)/shard_map/all_gather | solution.py:69
  582.9 2.2 fusion.174
  585.1 6.1 fusion
  591.2 37.7 %collective-permute-done.8 = f32[1024,288]{0,1:T(8,128)} collective-permute-done((f32[1024,288]{0,1:T(8,128)}, f32[1024,288]{0,1:T(8,128)}, u32[]{:S(2)}, u32[]{:S(2)}) %collective-permute-start.8) | collective-permute-done | bytes 1179680 | tf_op jit(solution)/shard_map/ppermute | solution.py:12
  628.9 2.6 bitcast_add_fusion
  631.8 1.9 fusion.38
  633.6 2.0 copy_bitcast_fusion.1
  635.6 3.3 gather_fusion.7
  639.0 3.0 fusion.41
  642.4 3.8 multiply_reduce_fusion.1
  646.2 14.7 %collective-permute-done.9 = f32[1024,288]{0,1:T(8,128)} collective-permute-done((f32[1024,288]{0,1:T(8,128)}, f32[1024,288]{0,1:T(8,128)}, u32[]{:S(2)}, u32[]{:S(2)}) %collective-permute-start.9) | collective-permute-done | bytes 1179680 | tf_op jit(solution)/shard_map/ppermute | solution.py:12
  660.9 3.1 multiply_reduce_fusion
  664.0 6.4 all-reduce.3
  671.2 3.8 convolution_bitcast_fusion.1
  675.0 3.5 convolution_bitcast_fusion
  680.4 682.5 %all-reduce.10.cloned.1.call-done = (f32[1152,288]{0,1:T(8,128)}, f32[1152,288]{0,1:T(8,128)}) async-done(((f32[1152,288]{0,1:T(8,128)}, f32[1152,288]{0,1:T(8,128)}), (f32[1152,288]{0,1:T(8,128)}, f32[1152,288]{0,1:T(8,128)})) %all-reduce.10.cloned.1.call-update) | async-done | bytes 2654224
  (139 shorter events, 48.9 us)
Async XLA Ops:
  7.2 1.7 copy-start
  7.2 50.2 %all-gather.6.cloned.1.call-start = ((), (), s32[]{:S(2)}) async-start(), calls=%async_computation.2 | async-start | bytes 2949120 | tf_op jit(solution)/shard_map/all_gather | solution.py:39
  8.8 3.2 copy-start.9
  8.8 3.2 copy-start.32
  20.2 44.2 %copy-start.16 = (f32[1024]{0:T(1024)}, f32[1024]{0:T(1024)S(1)}, u32[]{:S(2)}) copy-start(f32[1024]{0:T(1024)S(1)} %get-tuple-element.17) | copy-start | bytes 12292
  20.2 99.0 %copy-start.15 = (f32[1024]{0:T(1024)}, f32[1024]{0:T(1024)S(1)}, u32[]{:S(2)}) copy-start(f32[1024]{0:T(1024)S(1)} %get-tuple-element.16) | copy-start | bytes 12292
  21.1 103.5 %copy-start.24 = (s32[8,16]{1,0:T(8,128)S(1)}, s32[8,16]{1,0:T(8,128)}, u32[]{:S(2)}) copy-start(s32[8,16]{1,0:T(8,128)} %param.15) | copy-start | bytes 1540
  57.4 58.6 %collective-permute-start = (bf16[1024,1152]{0,1:T(8,128)(2,1)}, bf16[1024,1152]{0,1:T(8,128)(2,1)}, u32[]{:S(2)}, u32[]{:S(2)}) collective-permute-start(bf16[1024,1152]{0,1:T(8,128)(2,1)} %all-gather.6.cloned.1.call-done), channel_id=1, source_target_pairs={{0,248},{4,252},{8,0},{12,4},{16,8},{20,12},{24,16},{28,20},{32,24... | collective-permute-start | bytes 7077896 | tf_op jit(solution)/shard_map/ppermute | solution.py:12
  116.0 53.3 %collective-permute-start.1 = (bf16[1024,1152]{0,1:T(8,128)(2,1)}, bf16[1024,1152]{0,1:T(8,128)(2,1)}, u32[]{:S(2)}, u32[]{:S(2)}) collective-permute-start(bf16[1024,1152]{0,1:T(8,128)(2,1)} %collective-permute-done), channel_id=1, source_target_pairs={{0,4},{4,8},{8,12},{12,16},{16,20},{20,24},{24,28},{28,32},{32,36}... | collective-permute-start | bytes 7077896 | tf_op jit(solution)/shard_map/ppermute | solution.py:12
  117.4 0.8 copy-start.3
  119.1 13.7 %all-to-all-start = ((bf16[4,256,288]{1,2,0:T(8,128)(2,1)}), bf16[4,256,288]{1,2,0:T(8,128)(2,1)}, u32[]{:S(2)}, u32[]{:S(2)}) async-start(bf16[4,256,288]{1,2,0:T(8,128)(2,1)} %bitcast.192), calls=%async_computation | async-start | bytes 1179648 | tf_op jit(solution)/shard_map/all_to_all | solution.py:37
  123.3 151.9 %all-gather.8.cloned.1.call-start = ((), (), s32[]{:S(2)}) async-start(), calls=%async_computation.3 | async-start | bytes 1310720 | tf_op jit(solution)/shard_map/all_gather | solution.py:69
  125.4 0.6 copy-start.14
  151.8 163.2 %all-gather.10.cloned.1.call-start = ((), (), s32[]{:S(2)}) async-start(), calls=%async_computation.4 | async-start | bytes 1310720 | tf_op jit(solution)/shard_map/all_gather | solution.py:69
  169.3 85.4 %collective-permute-start.2 = (bf16[1024,1152]{0,1:T(8,128)(2,1)}, bf16[1024,1152]{0,1:T(8,128)(2,1)}, u32[]{:S(2)}, u32[]{:S(2)}) collective-permute-start(bf16[1024,1152]{0,1:T(8,128)(2,1)} %collective-permute-done.1), channel_id=1, source_target_pairs={{0,4},{4,8},{8,12},{12,16},{16,20},{20,24},{24,28},{28,32},{32,36}... | collective-permute-start | bytes 7077896 | tf_op jit(solution)/shard_map/ppermute | solution.py:12
  184.3 329.7 %all-reduce.8.cloned.1.call-start = ((), (), s32[]{:S(2)}) async-start(), calls=%async_computation.1 | async-start | bytes 8388608 | tf_op jit(solution)/shard_map/psum | solution.py:41
  188.9 359.8 %all-gather.12.cloned.1.call-start = ((), (), s32[]{:S(2)}) async-start(), calls=%async_computation.5 | async-start | bytes 1310720 | tf_op jit(solution)/shard_map/all_gather | solution.py:69
  254.7 60.1 %collective-permute-start.3 = (bf16[1024,1152]{0,1:T(8,128)(2,1)}, bf16[1024,1152]{0,1:T(8,128)(2,1)}, u32[]{:S(2)}, u32[]{:S(2)}) collective-permute-start(bf16[1024,1152]{0,1:T(8,128)(2,1)} %collective-permute-done.2), channel_id=1, source_target_pairs={{0,4},{4,8},{8,12},{12,16},{16,20},{20,24},{24,28},{28,32},{32,36}... | collective-permute-start | bytes 7077896 | tf_op jit(solution)/shard_map/ppermute | solution.py:12
  267.9 4.9 copy-start.30
  275.2 2.2 copy-start.23
  283.5 1.3 copy-start.26
  283.5 1.9 copy-start.25
  284.8 55.3 %collective-permute-start.5 = (f32[1024,288]{0,1:T(8,128)}, f32[1024,288]{0,1:T(8,128)}, u32[]{:S(2)}, u32[]{:S(2)}) collective-permute-start(f32[1024,288]{0,1:T(8,128)} %bitcast.159), channel_id=1, source_target_pairs={{0,4},{4,8},{8,12},{12,16},{16,20},{20,24},{24,28},{28,32},{32,36}... | collective-permute-start | bytes 3538952 | tf_op jit(solution)/shard_map/ppermute | solution.py:12
  286.6 30.6 %copy-start.22 = (s32[8,4]{0,1:T(4,128)S(1)}, s32[8,4]{0,1:T(4,128)}, u32[]{:S(2)}) copy-start(s32[8,4]{0,1:T(4,128)} %copy.114) | copy-start | bytes 388
  314.8 214.9 %collective-permute-start.4 = (bf16[1024,1152]{0,1:T(8,128)(2,1)}, bf16[1024,1152]{0,1:T(8,128)(2,1)}, u32[]{:S(2)}, u32[]{:S(2)}) collective-permute-start(bf16[1024,1152]{0,1:T(8,128)(2,1)} %collective-permute-done.3), channel_id=1, source_target_pairs={{0,4},{4,8},{8,12},{12,16},{16,20},{20,24},{24,28},{28,32},{32,36}... | collective-permute-start | bytes 7077896 | tf_op jit(solution)/shard_map/ppermute | solution.py:12
  342.8 185.1 %collective-permute-start.6 = (f32[1024,288]{0,1:T(8,128)}, f32[1024,288]{0,1:T(8,128)}, u32[]{:S(2)}, u32[]{:S(2)}) collective-permute-start(f32[1024,288]{0,1:T(8,128)} %bitcast_add_fusion.2), channel_id=1, source_target_pairs={{0,4},{4,8},{8,12},{12,16},{16,20},{20,24},{24,28},{28,32},{32,36}... | collective-permute-start | bytes 3538952 | tf_op jit(solution)/shard_map/ppermute | solution.py:12
  347.1 4.0 copy-start.31
  356.2 226.7 %all-gather.14.cloned.1.call-start = ((), (), s32[]{:S(2)}) async-start(), calls=%async_computation.6 | async-start | bytes 1310720 | tf_op jit(solution)/shard_map/all_gather | solution.py:69
  513.9 6.6 copy-start.19
  527.9 29.2 %collective-permute-start.7 = (f32[1024,288]{0,1:T(8,128)}, f32[1024,288]{0,1:T(8,128)}, u32[]{:S(2)}, u32[]{:S(2)}) collective-permute-start(f32[1024,288]{0,1:T(8,128)} %collective-permute-done.6), channel_id=1, source_target_pairs={{0,4},{4,8},{8,12},{12,16},{16,20},{20,24},{24,28},{28,32},{32,36}... | collective-permute-start | bytes 3538952 | tf_op jit(solution)/shard_map/ppermute | solution.py:12
  538.2 7.2 copy-start.18
  543.3 819.6 %all-reduce.10.cloned.1.call-start = ((), (), s32[]{:S(2)}) async-start(), calls=%async_computation.7 | async-start | bytes 5308416
  548.7 2.2 copy-start.21
  557.0 4.3 copy-start.8
  557.0 4.3 copy-start.12
  557.0 4.3 copy-start.29
  559.8 69.0 %collective-permute-start.8 = (f32[1024,288]{0,1:T(8,128)}, f32[1024,288]{0,1:T(8,128)}, u32[]{:S(2)}, u32[]{:S(2)}) collective-permute-start(f32[1024,288]{0,1:T(8,128)} %bitcast_add_fusion.1), channel_id=1, source_target_pairs={{0,4},{4,8},{8,12},{12,16},{16,20},{20,24},{24,28},{28,32},{32,36}... | collective-permute-start | bytes 3538952 | tf_op jit(solution)/shard_map/ppermute | solution.py:12
  561.3 3.9 copy-start.17
  568.5 16.6 %copy-start.20 = (s32[8,4]{0,1:T(4,128)S(1)}, s32[8,4]{0,1:T(4,128)}, u32[]{:S(2)}) copy-start(s32[8,4]{0,1:T(4,128)} %copy.120) | copy-start | bytes 388
  591.2 40.6 %copy-start.7 = (bf16[32,128,288]{1,2,0:T(8,128)(2,1)S(1)}, bf16[32,128,288]{1,2,0:T(8,128)(2,1)}, u32[]{:S(2)}) copy-start(bf16[32,128,288]{1,2,0:T(8,128)(2,1)} %gather_fusion.5) | copy-start | bytes 7077892
  591.2 40.6 %copy-start.13 = (bf16[8,4,128,128]{3,2,1,0:T(8,128)(2,1)S(1)}, bf16[8,4,128,128]{3,2,1,0:T(8,128)(2,1)}, u32[]{:S(2)}) copy-start(bf16[8,4,128,128]{3,2,1,0:T(8,128)(2,1)} %all-gather.12.cloned.1.call-done) | copy-start | bytes 3145732
  591.2 40.6 %copy-start.28 = (pred[8,4]{1,0:T(8,128)(4,1)S(1)}, pred[8,4]{1,0:T(8,128)(4,1)}, u32[]{:S(2)}) copy-start(pred[8,4]{1,0:T(8,128)(4,1)} %get-tuple-element.28) | copy-start | bytes 100
  631.5 29.4 %collective-permute-start.9 = (f32[1024,288]{0,1:T(8,128)}, f32[1024,288]{0,1:T(8,128)}, u32[]{:S(2)}, u32[]{:S(2)}) collective-permute-start(f32[1024,288]{0,1:T(8,128)} %bitcast_add_fusion), channel_id=1, source_target_pairs={{0,248},{4,252},{8,0},{12,4},{16,8},{20,12},{24,16},{28,20},{32,24... | collective-permute-start | bytes 3538952 | tf_op jit(solution)/shard_map/ppermute | solution.py:12
  635.6 3.3 copy-start.27
  638.9 3.0 copy-start.1
  638.9 3.0 copy-start.2
  638.9 3.1 copy-start.6
  639.0 3.5 copy-start.11
  642.4 18.5 %copy-start.4 = (bf16[1024,288]{0,1:T(8,128)(2,1)S(1)}, bf16[1024,288]{0,1:T(8,128)(2,1)}, u32[]{:S(2)}) copy-start(bf16[1024,288]{0,1:T(8,128)(2,1)} %copy-done.3) | copy-start | bytes 1769476
  671.2 3.9 copy-start.5
  671.2 3.9 copy-start.10
  678.5 0.7 copy-start.33
Sparse Core Ops, SparseCore 0:
  21.3 36.0 all-gather.5
  151.9 64.2 all-gather.7
  218.1 67.2 all-gather.9
  287.9 226.0 all-reduce.7
  515.6 23.7 all-gather.11
  543.4 39.3 all-gather.13
  678.7 684.2 all-reduce.9
where the time goes:
time: 1390 us; the launch traced here: 1370 us
  waiting for transfers between devices  1120 us (81%)
  local copies, waits for them, and re-layouts  93.9 us (7%)
  matrix products  79.9 us (6%)
  other arithmetic  29.7 us (2%)
  between operations  16.7 us (1%)
  starting transfers between devices  15.6 us (1%)
    unnamed x8, waiting for transfers between devices  683 us
    ppermute x10, waiting for transfers between devices, shifted(): return lax.ppermute(value, axis, pairs)  230 us
    psum x1, waiting for transfers between devices, shards(): scores = lax.psum(partial_value, 'mp')  158 us
    all_gather x1, waiting for transfers between devices, shards(): text_full = lax.all_gather(text_unit, 'mp', axis=1, tiled=True)  36.2 us
  transfers between devices with their start and end apart: 18, of which 12 were waited for; matrix products, arithmetic and copies ran while one was open for 13% of the time, Pallas kernels for 0%

commit v1 on v0

--- a/solution.py
+++ b/solution.py
@@ -1,25 +1,40 @@
 import jax
 import jax.numpy as jnp
 from jax import lax
-from jax.sharding import PartitionSpec as P
+from jax.sharding import Mesh, PartitionSpec as P
 
 EPSILON = 1e-06
 
 
+DP = ("yh", "z", "x")
+
+
 def shifted(value, axis, steps):
-    count = lax.axis_size(axis)
+    count = lax.psum(1, axis)
     pairs = [(source, (source + steps) % count) for source in range(count)]
     return lax.ppermute(value, axis, pairs)
+
+
+def reduce_rows(local_img, local_txt):
+    width = local_img.shape[1]
+    sizes = [lax.psum(1, axis) for axis in DP]
+    joined = jnp.concatenate([local_img, local_txt], axis=1)
+    rows = joined.shape[0] // (sizes[0] * sizes[1] * sizes[2])
+    joined = joined.reshape(sizes[0], sizes[1], sizes[2], rows, 2 * width)
+    for dim in (2, 1, 0):
+        joined = lax.all_to_all(joined, DP[dim], dim, dim, tiled=True).sum(dim, keepdims=True)
+    joined = joined.reshape(rows, 2 * width)
+    return joined[:, :width], joined[:, width:]
 
 
 def shards(image_feats, text_feats, image_head, text_head, hard_tiles, logit_scale, logit_bias):
     row_count = image_feats.shape[0]
     width_part = image_head.shape[1]
     per_block = row_count // 128
-    model_count = lax.axis_size("mp")
+    model_count = lax.psum(1, "mp")
     model_index = lax.axis_index("mp")
     tiles_share = per_block // model_count
-    span_blocks = min(2, (lax.axis_size("dp") - 1) // 2)
+    span_blocks = min(2, (lax.psum(1, DP) - 1) // 2)
     pick_count = hard_tiles.shape[1] // (2 * span_blocks)
     temp_scale = logit_scale[0]
     shift_bias = logit_bias[0]
@@ -45,12 +60,12 @@
     ).astype(jnp.bfloat16)
     grad_img = jnp.dot(weight, text_unit, preferred_element_type=jnp.float32)
     grad_txt = jnp.einsum("pq,pe->qe", weight, image_unit, preferred_element_type=jnp.float32)
-    current = shifted(text_full, "dp", -span_blocks)
+    current = shifted(text_full, DP, -span_blocks)
     carried = jnp.zeros_like(text_proj)
     for step_index in range(2 * span_blocks + 1):
         if step_index > 0:
-            current = shifted(current, "dp", 1)
-            carried = shifted(carried, "dp", 1)
+            current = shifted(current, DP, 1)
+            carried = shifted(carried, DP, 1)
         offset = span_blocks - step_index
         if offset != 0:
             slot_index = offset + span_blocks if offset < 0 else offset + span_blocks - 1
@@ -87,7 +102,7 @@
             )
             grad_img = grad_img + into_img
             carried = carried + into_txt
-    grad_txt = grad_txt + shifted(carried, "dp", -span_blocks)
+    grad_txt = grad_txt + shifted(carried, DP, -span_blocks)
     dots_img, dots_txt = lax.psum(
         (jnp.sum(image_proj * grad_img, axis=1), jnp.sum(text_proj * grad_txt, axis=1)), "mp"
     )
@@ -101,19 +116,23 @@
     )
     local_img = jnp.einsum("nd,ne->de", image_feats, dproj_img, preferred_element_type=jnp.float32)
     local_txt = jnp.einsum("nd,ne->de", text_feats, dproj_txt, preferred_element_type=jnp.float32)
-    head_grad_img, head_grad_txt = (
-        lax.psum_scatter(local_img, "dp", scatter_dimension=0, tiled=True),
-        lax.psum_scatter(local_txt, "dp", scatter_dimension=0, tiled=True),
-    )
+    head_grad_img, head_grad_txt = reduce_rows(local_img, local_txt)
     return (head_grad_img, head_grad_txt)
 
 
 def solution(mesh):
-    placed = (P("dp", None), P("dp", None), P(None, "mp"), P(None, "mp"), P("dp", None), P(), P())
+    dp_size = mesh.shape["dp"]
+    x_size = 4 if dp_size % 4 == 0 else 1
+    y_size = 2 if dp_size % (2 * x_size) == 0 and dp_size > 2 * x_size else 1
+    z_size = dp_size // (x_size * y_size)
+    split_mesh = Mesh(
+        mesh.devices.reshape(y_size, z_size, x_size, mesh.shape["mp"]), DP + ("mp",)
+    )
+    placed = (P(DP, None), P(DP, None), P(None, "mp"), P(None, "mp"), P(DP, None), P(), P())
     return jax.shard_map(
         shards,
-        mesh=mesh,
+        mesh=split_mesh,
         in_specs=placed,
-        out_specs=(P("dp", "mp"), P("dp", "mp")),
+        out_specs=(P(DP, "mp"), P(DP, "mp")),
         check_vma=False,
     )

time: 1390 us -> 786 us (0.57)
  waiting for transfers between devices: 1120 us -> 442 us
  blocking collectives: 13.6 us -> 85.3 us
    unnamed x8 -> x6, waiting for transfers between devices: 683 us -> 0.1 us
    all_to_all x0 -> x3, blocking collectives: none -> 71.8 us  [reduce_rows(): lax.all_to_all(joined, DP[dim], dim, dim, tiled=True)]
  transfers between devices with their start and end apart: 18 -> 17, of which waited for: 12 -> 11; matrix products, arithmetic and copies ran while one was open for 13% -> 23% of each run, Pallas kernels for 0% -> 0%
where the time goes in v1:
time: 786 us; the launch traced here: 776 us
  waiting for transfers between devices  442 us (56%)
  local copies, waits for them, and re-layouts  103 us (13%)
  blocking collectives  85.3 us (11%)
  matrix products  77.7 us (10%)
  other arithmetic  35.9 us (5%)
  between operations  16.3 us (2%)
  starting transfers between devices  15.6 us (2%)
    ppermute x10, waiting for transfers between devices, shifted(): return lax.ppermute(value, axis, pairs)  229 us
    psum x1, waiting for transfers between devices, shards(): scores = lax.psum(partial_value, 'mp')  158 us
    all_to_all x3, blocking collectives, reduce_rows(): lax.all_to_all(joined, DP[dim], dim, dim, tiled=True)  71.8 us
    all_gather x1, waiting for transfers between devices, shards(): text_full = lax.all_gather(text_unit, 'mp', axis=1, tiled=True)  36.2 us
    dot_general x4, matrix products, shards(): jnp.einsum('rkt,rkqe->tqe', onehot, into_sel, precision=lax.Precision.HIG...  24.5 us
    reshape x4, local copies, waits for them, and re-layouts, shards(): wide_tiles = current.reshape(per_block, 128, current.shape[1])  17.3 us
    gather x4, local copies, waits for them, and re-layouts, shards(): chosen_wide = jnp.take(wide_tiles, picked_mine, axis=0)  16.1 us
  transfers between devices with their start and end apart: 17, of which 11 were waited for; matrix products, arithmetic and copies ran while one was open for 23% of the time, Pallas kernels for 0%

profile of v1, /device:TPU:2, one launch (start us, length us, event | category | flops | bytes accessed | tf_op | source)
XLA Modules:
  0.0 775.8 jit_solution(6213469560428244813)
XLA Ops:
  8.8 3.2 multiply_reduce_fusion.3
  13.0 7.1 all-reduce.1
  21.2 36.2 %all-gather.6.cloned.1.call-done = bf16[1024,1152]{0,1:T(8,128)(2,1)} async-done(((bf16[1024,288]{0,1:T(8,128)(2,1)}), bf16[1024,1152]{0,1:T(8,128)(2,1)}) %all-gather.6.cloned.1.call-update) | async-done | bytes 2359312 | tf_op jit(solution)/shard_map/all_gather | solution.py:54
  57.4 7.0 collective-permute-start
  64.4 51.6 %collective-permute-done = bf16[1024,1152]{0,1:T(8,128)(2,1)} collective-permute-done((bf16[1024,1152]{0,1:T(8,128)(2,1)}, bf16[1024,1152]{0,1:T(8,128)(2,1)}, u32[]{:S(2)}, u32[]{:S(2)}) %collective-permute-start) | collective-permute-done | bytes 2359328 | tf_op jit(solution)/shard_map/ppermute | solution.py:15
  119.2 4.1 all-to-all-start
  129.1 3.8 all-to-all-done
  132.9 2.5 reshape.88
  135.4 2.9 copy.194
  138.4 4.4 copy.210
  142.7 4.0 gather_fusion
  146.8 3.3 fusion.160
  154.5 14.8 %collective-permute-done.1 = bf16[1024,1152]{0,1:T(8,128)(2,1)} collective-permute-done((bf16[1024,1152]{0,1:T(8,128)(2,1)}, bf16[1024,1152]{0,1:T(8,128)(2,1)}, u32[]{:S(2)}, u32[]{:S(2)}) %collective-permute-start.1) | collective-permute-done | bytes 2359328 | tf_op jit(solution)/shard_map/ppermute | solution.py:15
  170.8 4.3 copy.213
  175.1 4.0 gather_fusion.2
  179.1 3.3 fusion.148
  184.3 4.6 fusion.198
  188.9 65.8 %collective-permute-done.2 = bf16[1024,1152]{0,1:T(8,128)(2,1)} collective-permute-done((bf16[1024,1152]{0,1:T(8,128)(2,1)}, bf16[1024,1152]{0,1:T(8,128)(2,1)}, u32[]{:S(2)}, u32[]{:S(2)}) %collective-permute-start.2) | collective-permute-done | bytes 2359328 | tf_op jit(solution)/shard_map/ppermute | solution.py:15
  275.3 2.2 fusion.168
  277.5 6.1 fusion.6
  286.7 28.2 %collective-permute-done.3 = bf16[1024,1152]{0,1:T(8,128)(2,1)} collective-permute-done((bf16[1024,1152]{0,1:T(8,128)(2,1)}, bf16[1024,1152]{0,1:T(8,128)(2,1)}, u32[]{:S(2)}, u32[]{:S(2)}) %collective-permute-start.3) | collective-permute-done | bytes 2359328 | tf_op jit(solution)/shard_map/ppermute | solution.py:15
  315.4 2.2 fusion.170
  317.5 6.1 fusion.4
  323.7 16.6 %collective-permute-done.5 = f32[1024,288]{0,1:T(8,128)} collective-permute-done((f32[1024,288]{0,1:T(8,128)}, f32[1024,288]{0,1:T(8,128)}, u32[]{:S(2)}, u32[]{:S(2)}) %collective-permute-start.5) | collective-permute-done | bytes 1179680 | tf_op jit(solution)/shard_map/ppermute | solution.py:15
  340.2 2.7 bitcast_add_fusion.2
  342.9 4.3 copy.216
  347.2 4.0 gather_fusion.4
  351.2 3.3 fusion.136
  356.4 157.6 %all-reduce.4.cloned.1.call-done = f32[1024,1024]{1,0:T(8,128)} async-done(((f32[1024,1024]{1,0:T(8,128)}), f32[1024,1024]{1,0:T(8,128)}) %all-reduce.4.cloned.1.call-update) | async-done | bytes 4194320 | tf_op jit(solution)/shard_map/psum | solution.py:56
  514.0 4.7 multiply_convert_fusion
  518.7 2.0 copy_bitcast_fusion.4
  520.7 3.4 gather_fusion.1
  524.1 3.8 fusion.32
  529.6 4.3 copy.219
  533.9 4.1 gather_fusion.6
  538.0 3.3 fusion.124
  543.2 2.0 copy_bitcast_fusion.3
  545.2 3.3 gather_fusion.3
  548.5 2.2 fusion.172
  550.7 6.1 fusion.2
  556.8 2.8 bitcast_add_fusion.1
  563.0 2.0 copy_bitcast_fusion.2
  565.0 3.3 gather_fusion.5
  568.3 14.6 %all-gather.14.cloned.1.call-done = bf16[8,4,128,128]{3,2,1,0:T(8,128)(2,1)} async-done(((bf16[2,4,128,128]{3,2,1,0:T(8,128)(2,1)}), bf16[8,4,128,128]{3,2,1,0:T(8,128)(2,1)}) %all-gather.14.cloned.1.call-update) | async-done | bytes 1048592 | tf_op jit(solution)/shard_map/all_gather | solution.py:84
  582.9 2.2 fusion.174
  585.1 6.1 fusion
  591.2 37.8 %collective-permute-done.8 = f32[1024,288]{0,1:T(8,128)} collective-permute-done((f32[1024,288]{0,1:T(8,128)}, f32[1024,288]{0,1:T(8,128)}, u32[]{:S(2)}, u32[]{:S(2)}) %collective-permute-start.8) | collective-permute-done | bytes 1179680 | tf_op jit(solution)/shard_map/ppermute | solution.py:15
  629.0 2.6 bitcast_add_fusion
  633.8 2.0 copy_bitcast_fusion.1
  635.8 3.3 gather_fusion.7
  639.2 2.9 fusion.41
  642.6 3.9 multiply_reduce_fusion.1
  646.5 14.6 %collective-permute-done.9 = f32[1024,288]{0,1:T(8,128)} collective-permute-done((f32[1024,288]{0,1:T(8,128)}, f32[1024,288]{0,1:T(8,128)}, u32[]{:S(2)}, u32[]{:S(2)}) %collective-permute-start.9) | collective-permute-done | bytes 1179680 | tf_op jit(solution)/shard_map/ppermute | solution.py:15
  661.1 3.1 multiply_reduce_fusion
  664.2 6.4 all-reduce
  671.4 2.7 convolution_bitcast_fusion.1
  674.1 2.4 convolution_bitcast_fusion
  678.2 3.5 copy.190
  681.7 4.5 reshape.105
  686.2 3.8 copy.191
  690.0 37.1 %all_to_all.31 = f32[2,8,4,18,576]{4,1,3,0,2:T(8,128)} all-to-all(f32[2,8,4,18,576]{4,1,3,0,2:T(8,128)S(1)} %copy.191), channel_id=1, replica_groups=mesh['yh'=2,'z'=8,'x'=4,'mp'=4] {'x'}, dimensions={2} | all-to-all | bytes 5308416 | tf_op jit(solution)/shard_map/all_to_all | solution.py:25
  727.1 3.0 reduce_sum.67
  731.6 26.5 %all_to_all.32 = f32[2,8,1,18,576]{4,0,3,2,1:T(2,128)} all-to-all(f32[2,8,1,18,576]{4,0,3,2,1:T(2,128)S(1)} %copy.192), channel_id=1, replica_groups=mesh['yh'=2,'z'=8,'x'=4,'mp'=4] {'z'}, dimensions={1} | all-to-all | bytes 1327104 | tf_op jit(solution)/shard_map/all_to_all | solution.py:25
  759.6 8.1 %all_to_all.33 = f32[2,1,1,18,576]{4,2,3,1,0:T(1,128)S(1)} all-to-all(f32[2,1,1,18,576]{4,2,3,1,0:T(1,128)S(1)} %copy.193), channel_id=1, replica_groups=mesh['yh'=2,'z'=8,'x'=4,'mp'=4] {'yh'}, dimensions={0} | all-to-all | bytes 165888 | tf_op jit(solution)/shard_map/all_to_all | solution.py:25
  (142 shorter events, 60.5 us)
Async XLA Ops:
  7.2 1.7 copy-start
  7.2 50.2 %all-gather.6.cloned.1.call-start = ((), (), s32[]{:S(2)}) async-start(), calls=%async_computation.5 | async-start | bytes 2949120 | tf_op jit(solution)/shard_map/all_gather | solution.py:54
  8.8 3.2 copy-start.9
  8.8 3.2 copy-start.32
  20.2 44.2 %copy-start.16 = (f32[1024]{0:T(1024)}, f32[1024]{0:T(1024)S(1)}, u32[]{:S(2)}) copy-start(f32[1024]{0:T(1024)S(1)} %get-tuple-element.7) | copy-start | bytes 12292
  20.2 99.0 %copy-start.15 = (f32[1024]{0:T(1024)}, f32[1024]{0:T(1024)S(1)}, u32[]{:S(2)}) copy-start(f32[1024]{0:T(1024)S(1)} %get-tuple-element.6) | copy-start | bytes 12292
  21.1 103.5 %copy-start.24 = (s32[8,16]{1,0:T(8,128)S(1)}, s32[8,16]{1,0:T(8,128)}, u32[]{:S(2)}) copy-start(s32[8,16]{1,0:T(8,128)} %param.15) | copy-start | bytes 1540
  57.4 58.6 %collective-permute-start = (bf16[1024,1152]{0,1:T(8,128)(2,1)}, bf16[1024,1152]{0,1:T(8,128)(2,1)}, u32[]{:S(2)}, u32[]{:S(2)}) collective-permute-start(bf16[1024,1152]{0,1:T(8,128)(2,1)} %all-gather.6.cloned.1.call-done), channel_id=1, source_target_pairs={{0,248},{4,252},{8,0},{12,4},{16,8},{20,12},{24,16},{28,20},{32,24... | collective-permute-start | bytes 7077896 | tf_op jit(solution)/shard_map/ppermute | solution.py:15
  116.0 53.3 %collective-permute-start.1 = (bf16[1024,1152]{0,1:T(8,128)(2,1)}, bf16[1024,1152]{0,1:T(8,128)(2,1)}, u32[]{:S(2)}, u32[]{:S(2)}) collective-permute-start(bf16[1024,1152]{0,1:T(8,128)(2,1)} %collective-permute-done), channel_id=1, source_target_pairs={{0,4},{4,8},{8,12},{12,16},{16,20},{20,24},{24,28},{28,32},{32,36}... | collective-permute-start | bytes 7077896 | tf_op jit(solution)/shard_map/ppermute | solution.py:15
  117.4 0.8 copy-start.3
  119.2 13.7 %all-to-all-start = ((bf16[4,256,288]{1,2,0:T(8,128)(2,1)}), bf16[4,256,288]{1,2,0:T(8,128)(2,1)}, u32[]{:S(2)}, u32[]{:S(2)}) async-start(bf16[4,256,288]{1,2,0:T(8,128)(2,1)} %bitcast.190), calls=%async_computation | async-start | bytes 1179648 | tf_op jit(solution)/shard_map/all_to_all | solution.py:52
  123.3 151.9 %all-gather.8.cloned.1.call-start = ((), (), s32[]{:S(2)}) async-start(), calls=%async_computation.6 | async-start | bytes 1310720 | tf_op jit(solution)/shard_map/all_gather | solution.py:84
  125.4 0.6 copy-start.14
  151.9 163.5 %all-gather.10.cloned.1.call-start = ((), (), s32[]{:S(2)}) async-start(), calls=%async_computation.7 | async-start | bytes 1310720 | tf_op jit(solution)/shard_map/all_gather | solution.py:84
  169.3 85.5 %collective-permute-start.2 = (bf16[1024,1152]{0,1:T(8,128)(2,1)}, bf16[1024,1152]{0,1:T(8,128)(2,1)}, u32[]{:S(2)}, u32[]{:S(2)}) collective-permute-start(bf16[1024,1152]{0,1:T(8,128)(2,1)} %collective-permute-done.1), channel_id=1, source_target_pairs={{0,4},{4,8},{8,12},{12,16},{16,20},{20,24},{24,28},{28,32},{32,36}... | collective-permute-start | bytes 7077896 | tf_op jit(solution)/shard_map/ppermute | solution.py:15
  184.3 329.8 %all-reduce.4.cloned.1.call-start = ((), (), s32[]{:S(2)}) async-start(), calls=%async_computation.4 | async-start | bytes 8388608 | tf_op jit(solution)/shard_map/psum | solution.py:56
  188.9 359.6 %all-gather.12.cloned.1.call-start = ((), (), s32[]{:S(2)}) async-start(), calls=%async_computation.8 | async-start | bytes 1310720 | tf_op jit(solution)/shard_map/all_gather | solution.py:84
  254.8 60.2 %collective-permute-start.3 = (bf16[1024,1152]{0,1:T(8,128)(2,1)}, bf16[1024,1152]{0,1:T(8,128)(2,1)}, u32[]{:S(2)}, u32[]{:S(2)}) collective-permute-start(bf16[1024,1152]{0,1:T(8,128)(2,1)} %collective-permute-done.2), channel_id=1, source_target_pairs={{0,4},{4,8},{8,12},{12,16},{16,20},{20,24},{24,28},{28,32},{32,36}... | collective-permute-start | bytes 7077896 | tf_op jit(solution)/shard_map/ppermute | solution.py:15
  267.9 4.9 copy-start.30
  275.3 2.2 copy-start.23
  283.6 1.3 copy-start.26
  283.6 1.8 copy-start.25
  284.8 55.4 %collective-permute-start.5 = (f32[1024,288]{0,1:T(8,128)}, f32[1024,288]{0,1:T(8,128)}, u32[]{:S(2)}, u32[]{:S(2)}) collective-permute-start(f32[1024,288]{0,1:T(8,128)} %bitcast.156), channel_id=1, source_target_pairs={{0,4},{4,8},{8,12},{12,16},{16,20},{20,24},{24,28},{28,32},{32,36}... | collective-permute-start | bytes 3538952 | tf_op jit(solution)/shard_map/ppermute | solution.py:15
  286.7 30.8 %copy-start.22 = (s32[8,4]{0,1:T(4,128)S(1)}, s32[8,4]{0,1:T(4,128)}, u32[]{:S(2)}) copy-start(s32[8,4]{0,1:T(4,128)} %copy.181) | copy-start | bytes 388
  314.9 214.6 %collective-permute-start.4 = (bf16[1024,1152]{0,1:T(8,128)(2,1)}, bf16[1024,1152]{0,1:T(8,128)(2,1)}, u32[]{:S(2)}, u32[]{:S(2)}) collective-permute-start(bf16[1024,1152]{0,1:T(8,128)(2,1)} %collective-permute-done.3), channel_id=1, source_target_pairs={{0,4},{4,8},{8,12},{12,16},{16,20},{20,24},{24,28},{28,32},{32,36}... | collective-permute-start | bytes 7077896 | tf_op jit(solution)/shard_map/ppermute | solution.py:15
  342.9 185.0 %collective-permute-start.6 = (f32[1024,288]{0,1:T(8,128)}, f32[1024,288]{0,1:T(8,128)}, u32[]{:S(2)}, u32[]{:S(2)}) collective-permute-start(f32[1024,288]{0,1:T(8,128)} %bitcast_add_fusion.2), channel_id=1, source_target_pairs={{0,4},{4,8},{8,12},{12,16},{16,20},{20,24},{24,28},{28,32},{32,36}... | collective-permute-start | bytes 3538952 | tf_op jit(solution)/shard_map/ppermute | solution.py:15
  347.2 4.0 copy-start.31
  356.3 226.6 %all-gather.14.cloned.1.call-start = ((), (), s32[]{:S(2)}) async-start(), calls=%async_computation.9 | async-start | bytes 1310720 | tf_op jit(solution)/shard_map/all_gather | solution.py:84
  514.0 6.7 copy-start.19
  527.9 28.9 %collective-permute-start.7 = (f32[1024,288]{0,1:T(8,128)}, f32[1024,288]{0,1:T(8,128)}, u32[]{:S(2)}, u32[]{:S(2)}) collective-permute-start(f32[1024,288]{0,1:T(8,128)} %collective-permute-done.6), channel_id=1, source_target_pairs={{0,4},{4,8},{8,12},{12,16},{16,20},{20,24},{24,28},{28,32},{32,36}... | collective-permute-start | bytes 3538952 | tf_op jit(solution)/shard_map/ppermute | solution.py:15
  538.0 7.1 copy-start.18
  548.5 2.2 copy-start.21
  556.8 4.4 copy-start.8
  556.8 4.4 copy-start.12
  556.8 4.4 copy-start.29
  559.6 69.4 %collective-permute-start.8 = (f32[1024,288]{0,1:T(8,128)}, f32[1024,288]{0,1:T(8,128)}, u32[]{:S(2)}, u32[]{:S(2)}) collective-permute-start(f32[1024,288]{0,1:T(8,128)} %bitcast_add_fusion.1), channel_id=1, source_target_pairs={{0,4},{4,8},{8,12},{12,16},{16,20},{20,24},{24,28},{28,32},{32,36}... | collective-permute-start | bytes 3538952 | tf_op jit(solution)/shard_map/ppermute | solution.py:15
  561.2 3.8 copy-start.17
  568.3 16.8 %copy-start.20 = (s32[8,4]{0,1:T(4,128)S(1)}, s32[8,4]{0,1:T(4,128)}, u32[]{:S(2)}) copy-start(s32[8,4]{0,1:T(4,128)} %copy.187) | copy-start | bytes 388
  591.2 40.7 %copy-start.7 = (bf16[32,128,288]{1,2,0:T(8,128)(2,1)S(1)}, bf16[32,128,288]{1,2,0:T(8,128)(2,1)}, u32[]{:S(2)}) copy-start(bf16[32,128,288]{1,2,0:T(8,128)(2,1)} %gather_fusion.5) | copy-start | bytes 7077892
  591.2 40.7 %copy-start.13 = (bf16[8,4,128,128]{3,2,1,0:T(8,128)(2,1)S(1)}, bf16[8,4,128,128]{3,2,1,0:T(8,128)(2,1)}, u32[]{:S(2)}) copy-start(bf16[8,4,128,128]{3,2,1,0:T(8,128)(2,1)} %all-gather.12.cloned.1.call-done) | copy-start | bytes 3145732
  591.2 40.7 %copy-start.28 = (pred[8,4]{1,0:T(8,128)(4,1)S(1)}, pred[8,4]{1,0:T(8,128)(4,1)}, u32[]{:S(2)}) copy-start(pred[8,4]{1,0:T(8,128)(4,1)} %get-tuple-element.20) | copy-start | bytes 100
  631.7 29.4 %collective-permute-start.9 = (f32[1024,288]{0,1:T(8,128)}, f32[1024,288]{0,1:T(8,128)}, u32[]{:S(2)}, u32[]{:S(2)}) collective-permute-start(f32[1024,288]{0,1:T(8,128)} %bitcast_add_fusion), channel_id=1, source_target_pairs={{0,248},{4,252},{8,0},{12,4},{16,8},{20,12},{24,16},{28,20},{32,24... | collective-permute-start | bytes 3538952 | tf_op jit(solution)/shard_map/ppermute | solution.py:15
  635.8 3.3 copy-start.27
  639.1 3.0 copy-start.1
  639.1 3.0 copy-start.2
  639.2 3.1 copy-start.6
  639.2 3.5 copy-start.11
  642.6 18.5 %copy-start.4 = (bf16[1024,288]{0,1:T(8,128)(2,1)S(1)}, bf16[1024,288]{0,1:T(8,128)(2,1)}, u32[]{:S(2)}) copy-start(bf16[1024,288]{0,1:T(8,128)(2,1)} %copy-done.3) | copy-start | bytes 1769476
  671.3 2.8 copy-start.5
  671.3 2.8 copy-start.10
Sparse Core Ops, SparseCore 0:
  21.3 36.0 all-gather.5
  152.0 64.2 all-gather.7
  218.1 67.2 all-gather.9
  287.9 226.0 all-reduce.3
  515.7 23.7 all-gather.11
  543.3 39.5 all-gather.13

commit v2 on v1

v2 whole, which is shorter than its diff:
```python
import jax
import jax.numpy as jnp
from jax import lax
from jax.sharding import Mesh, PartitionSpec as P

EPSILON = 1e-06
DP = ("yh", "z", "x")
ALL = DP + ("mp",)


def shifted(value, axis, steps):
    count = lax.psum(1, axis)
    pairs = [(source, (source + steps) % count) for source in range(count)]
    return lax.ppermute(value, axis, pairs)


def reduce_rows(local_img, local_txt):
    width = local_img.shape[1]
    sizes = [lax.psum(1, axis) for axis in DP]
    joined = jnp.concatenate([local_img, local_txt], axis=1)
    rows = joined.shape[0] // (sizes[0] * sizes[1] * sizes[2])
    joined = joined.reshape(sizes[0], sizes[1], sizes[2], rows, 2 * width)
    for dim in (2, 1, 0):
        joined = lax.all_to_all(joined, DP[dim], dim, dim, tiled=True).sum(dim, keepdims=True)
    joined = joined.reshape(rows, 2 * width)
    return joined[:, :width], joined[:, width:]


def embed(features, head):
    projected = jnp.dot(features, head, preferred_element_type=jnp.float32)
    inverse = lax.rsqrt(jnp.sum(projected * projected, axis=1) + EPSILON)
    unit = (projected * inverse[:, None]).astype(jnp.bfloat16)
    return projected, inverse, unit


def shards(image_feats, text_feats, image_head, text_head, hard_tiles, logit_scale, logit_bias):
    row_count = image_feats.shape[0]
    width_part = image_head.shape[1]
    per_block = row_count // 128
    model_count = lax.psum(1, "mp")
    model_index = lax.axis_index("mp")
    block_count = lax.psum(1, DP)
    share = row_count // model_count
    offsets = (-2, -1, 1, 2)
    slot_of_model = (0, 2, 1, 3)
    model_of_slot = tuple(slot_of_model.index(s) for s in range(4))
    pick_count = hard_tiles.shape[1] // len(offsets)
    temp_scale = logit_scale[0]
    shift_bias = logit_bias[0]

    head_img, head_txt = lax.all_gather((image_head, text_head), "mp", axis=1, tiled=True)
    image_proj, inverse_img, image_unit = embed(image_feats, head_img)
    text_proj, inverse_txt, text_unit = embed(text_feats, head_txt)

    pairs = []
    for block in range(block_count):
        for model in range(model_count):
            source = ((block + offsets[slot_of_model[model]]) % block_count) * model_count + model
            pairs.append((source, block * model_count + model))
    text_near = lax.ppermute(text_unit, ALL, pairs)

    local_ids = hard_tiles % per_block
    my_slot = jnp.array(slot_of_model, jnp.int32)[model_index]
    my_picks = lax.dynamic_slice_in_dim(local_ids, my_slot * pick_count, pick_count, 1)
    image_tiles_full = image_unit.reshape(per_block, 128, image_unit.shape[1])
    near_tiles = text_near.reshape(per_block, 128, text_near.shape[1])
    chosen_full = jnp.take(near_tiles, my_picks, axis=0)
    pair_scores = jnp.einsum(
        "rpe,rkqe->rkpq", image_tiles_full, chosen_full, preferred_element_type=jnp.float32
    )
    hard_weight = (temp_scale * jax.nn.sigmoid(temp_scale * pair_scores + shift_bias)).astype(
        jnp.bfloat16
    )

    image_mine = lax.dynamic_slice_in_dim(image_unit, model_index * share, share, 0)
    own_scores = jnp.dot(image_mine, text_unit.T, preferred_element_type=jnp.float32)
    diagonal_mask = (
        jnp.arange(row_count, dtype=jnp.int32)[None, :]
        == (jnp.arange(share, dtype=jnp.int32) + model_index * share)[:, None]
    ).astype(jnp.float32)
    own_weight = (
        temp_scale * (jax.nn.sigmoid(temp_scale * own_scores + shift_bias) - diagonal_mask)
    ).astype(jnp.bfloat16)

    own_size = own_weight.size
    packed = jnp.concatenate([own_weight.reshape(-1), hard_weight.reshape(-1)])
    gathered = lax.all_gather(packed, "mp", axis=0, tiled=False)
    weight = gathered[:, :own_size].reshape(row_count, row_count)
    hard_all = gathered[:, own_size:].reshape((model_count,) + hard_weight.shape)

    text_split = text_near.reshape(row_count, model_count, width_part)
    text_split = lax.all_to_all(text_split, "mp", 1, 1, tiled=True)

    e_start = model_index * width_part
    text_local = lax.dynamic_slice_in_dim(text_unit, e_start, width_part, 1)
    image_local = lax.dynamic_slice_in_dim(image_unit, e_start, width_part, 1)
    proj_img = lax.dynamic_slice_in_dim(image_proj, e_start, width_part, 1)
    proj_txt = lax.dynamic_slice_in_dim(text_proj, e_start, width_part, 1)
    image_tiles = image_local.reshape(per_block, 128, width_part)

    grad_img = jnp.dot(weight, text_local, preferred_element_type=jnp.float32)
    grad_txt = jnp.einsum("pq,pe->qe", weight, image_local, preferred_element_type=jnp.float32)
    for slot, offset in enumerate(offsets):
        source_model = model_of_slot[slot]
        pair_weight = hard_all[source_model]
        picked = local_ids[:, pick_count * slot : pick_count * slot + pick_count]
        near_local = text_split[:, source_model, :].reshape(per_block, 128, width_part)
        chosen = jnp.take(near_local, picked, axis=0)
        into_img = jnp.einsum(
            "rkpq,rkqe->rpe", pair_weight, chosen, preferred_element_type=jnp.float32
        )
        into_sel = jnp.einsum(
            "rkpq,rpe->rkqe", pair_weight, image_tiles, preferred_element_type=jnp.float32
        )
        onehot = (
            picked[:, :, None] == jnp.arange(per_block, dtype=jnp.int32)[None, None, :]
        ).astype(jnp.float32)
        into_txt = jnp.einsum("rkt,rkqe->tqe", onehot, into_sel, precision=lax.Precision.HIGHEST)
        grad_img = grad_img + into_img.reshape(row_count, width_part)
        grad_txt = grad_txt + shifted(into_txt.reshape(row_count, width_part), DP, offset)

    dots_img, dots_txt = lax.psum(
        (jnp.sum(proj_img * grad_img, axis=1), jnp.sum(proj_txt * grad_txt, axis=1)), "mp"
    )
    cube_img = dots_img * inverse_img * inverse_img * inverse_img
    cube_txt = dots_txt * inverse_txt * inverse_txt * inverse_txt
    dproj_img = (inverse_img[:, None] * grad_img - cube_img[:, None] * proj_img).astype(
        jnp.bfloat16
    )
    dproj_txt = (inverse_txt[:, None] * grad_txt - cube_txt[:, None] * proj_txt).astype(
        jnp.bfloat16
    )
    local_img = jnp.einsum("nd,ne->de", image_feats, dproj_img, preferred_element_type=jnp.float32)
    local_txt = jnp.einsum("nd,ne->de", text_feats, dproj_txt, preferred_element_type=jnp.float32)
    return reduce_rows(local_img, local_txt)


def solution(mesh):
    dp_size = mesh.shape["dp"]
    x_size = 4 if dp_size % 4 == 0 else 1
    y_size = 2 if dp_size % (2 * x_size) == 0 and dp_size > 2 * x_size else 1
    z_size = dp_size // (x_size * y_size)
    split_mesh = Mesh(
        mesh.devices.reshape(y_size, z_size, x_size, mesh.shape["mp"]), DP + ("mp",)
    )
    placed = (P(DP, None), P(DP, None), P(None, "mp"), P(None, "mp"), P(DP, None), P(), P())
    return jax.shard_map(
        shards,
        mesh=split_mesh,
        in_specs=placed,
        out_specs=(P(DP, "mp"), P(DP, "mp")),
        check_vma=False,
    )
```

time: 786 us -> 507 us (0.65)
  waiting for transfers between devices: 442 us -> 187 us
  other arithmetic: 35.9 us -> 9.81 us
  local copies, waits for them, and re-layouts: 103 us -> 113 us
    ppermute x10 -> x4, waiting for transfers between devices: 229 us -> 46.6 us  [shifted(): return lax.ppermute(value, axis, pairs)]
    psum x1 -> x0, waiting for transfers between devices: 158 us -> none  [shards(): scores = lax.psum(partial_value, 'mp')]
    all_gather x5 -> x3, waiting for transfers between devices: 50.9 us -> 98.4 us  [the longest x2 88.5 us: shards(): lax.all_gather((image_head, text_head), 'mp', axis=1, tiled=True)]
    all_to_all x1, waiting for transfers between devices: 3.83 us -> 40.9 us  [shards(): text_split = lax.all_to_all(text_split, 'mp', 1, 1, tiled=True)]
    slice x4 -> x6, local copies, waits for them, and re-layouts: 4.59 us -> 33.7 us  [the longest x1 28.8 us: shards(): pair_weight = hard_all[source_model]]
    reshape x10 -> x1, local copies, waits for them, and re-layouts: 30.7 us -> 4.78 us  [shards(): weight = gathered[:, :own_size].reshape(row_count, row_count)]
    unnamed x68 -> x47, local copies, waits for them, and re-layouts: 5.78 us -> 16.6 us
    broadcast_in_dim x8 -> x5, local copies, waits for them, and re-layouts: 10.3 us -> 0.39 us  [the longest x4 0.32 us: shards(): chosen = jnp.take(near_local, picked, axis=0)]
  transfers between devices with their start and end apart: 17 -> 9, of which waited for: 11 -> 6; matrix products, arithmetic and copies ran while one was open for 23% -> 19% of each run, Pallas kernels for 0% -> 0%
where the time goes in v2:
time: 507 us; the launch traced here: 497 us
  waiting for transfers between devices  187 us (37%)
  local copies, waits for them, and re-layouts  113 us (22%)
  blocking collectives  78.4 us (15%)
  matrix products  72.8 us (14%)
  starting transfers between devices  20 us (4%)
  between operations  16.4 us (3%)
  other arithmetic  9.81 us (2%)
    all_gather x2, waiting for transfers between devices, shards(): lax.all_gather((image_head, text_head), 'mp', axis=1, tiled=True)  88.5 us
    all_to_all x3, blocking collectives, reduce_rows(): lax.all_to_all(joined, DP[dim], dim, dim, tiled=True)  72.3 us
    ppermute x4, waiting for transfers between devices, shifted(): return lax.ppermute(value, axis, pairs)  46.6 us
    all_to_all x1, waiting for transfers between devices, shards(): text_split = lax.all_to_all(text_split, 'mp', 1, 1, tiled=True)  40.9 us
    slice x1, local copies, waits for them, and re-layouts, shards(): pair_weight = hard_all[source_model]  28.8 us
    dot_general x4, matrix products, shards(): jnp.einsum('rkt,rkqe->tqe', onehot, into_sel, precision=lax.Precision.HIG...  24.5 us
    unnamed x47, local copies, waits for them, and re-layouts  16.6 us
    gather x4, local copies, waits for them, and re-layouts, shards(): chosen = jnp.take(near_local, picked, axis=0)  13.3 us
  transfers between devices with their start and end apart: 9, of which 6 were waited for; matrix products, arithmetic and copies ran while one was open for 19% of the time, Pallas kernels for 0%

profile of v2, /device:TPU:2, one launch (start us, length us, event | category | flops | bytes accessed | tf_op | source)
XLA Modules:
  0.0 497.4 jit_solution(1612899707778432626)
XLA Ops:
  8.7 1.2 dynamic_slice.22
  11.3 37.3 %all-gather.7.cloned.1.call-done = bf16[1152,1152]{0,1:T(8,128)(2,1)} async-done(((bf16[1152,288]{0,1:T(8,128)(2,1)}), bf16[1152,1152]{0,1:T(8,128)(2,1)}) %all-gather.7.cloned.1.call-update) | async-done | bytes 2654224 | tf_op jit(solution)/shard_map/all_gather | solution.py:51
  48.6 5.4 %multiply_reduce_fusion = (f32[1024]{0:T(1024)S(1)}, f32[1024,1152]{1,0:T(8,128)S(1)}) fusion(bf16[1024,1152]{1,0:T(8,128)(2,1)S(1)} %copy-done, bf16[1152,1152]{0,1:T(8,128)(2,1)} %all-gather.7.cloned.1.call-done), kind=kOutput, calls=%fused_computation.18 | convolution fusion | flops 2720267264 | bytes 9736192 | tf_op jit(solution)/shard_map/dot_general | solution.py:30
  54.0 2.0 multiply_convert_fusion
  56.0 0.8 copy-done.4
  56.8 2.1 collective-permute-start
  60.4 51.2 %all-gather.5.cloned.1.call-done = bf16[1152,1152]{0,1:T(8,128)(2,1)} async-done(((bf16[1152,288]{0,1:T(8,128)(2,1)}), bf16[1152,1152]{0,1:T(8,128)(2,1)}) %all-gather.5.cloned.1.call-update) | async-done | bytes 2654224 | tf_op jit(solution)/shard_map/all_gather | solution.py:51
  111.6 6.1 %multiply_reduce_fusion.1 = (f32[1024]{0:T(1024)S(1)}, f32[1024,1152]{1,0:T(8,128)S(1)}) fusion(bf16[1024,1152]{1,0:T(8,128)(2,1)} %param.10, bf16[1152,1152]{0,1:T(8,128)(2,1)} %all-gather.5.cloned.1.call-done), kind=kOutput, calls=%fused_computation.20 | convolution fusion | flops 2720267264 | bytes 9736192 | tf_op jit(solution)/shard_map/dot_general | solution.py:30
  118.1 1.7 copy-done.3
  119.8 3.6 fusion.40
  123.4 0.9 copy.197
  124.3 7.3 %gather_fusion = bf16[32,128,1152]{2,1,0:T(8,128)(2,1)} fusion(bf16[8,128,1152]{2,1,0:T(8,128)(2,1)} %bitcast.3, s32[1024]{0:T(1024)S(1)} %pad_clamp_fusion.4), kind=kCustom, calls=%fused_computation.4 | custom fusion | bytes 18874496 | tf_op jit(solution)/shard_map/jit(_take)/gather | solution.py:67
  131.6 8.1 %fusion.28 = bf16[8,4,128,128]{2,3,1,0:T(8,128)(2,1)} fusion(bf16[8,128,1152,1]{2,1,3,0:T(8,128)(2,1)} %bitcast.169, bf16[8,4,128,1152]{3,2,1,0:T(8,128)(2,1)} %bitcast.163, pred[8,4]{1,0:T(8,128)(4,1)S(1)} %get-tuple-element.21, f32[]{:T(128)} %bitcast.156, f32[]{:T(128)} %bitcast.158), kind=kOutput, calls=%fused_computation.51 | convolution fusion | flops 1216348160 | bytes 12845096 | tf_op jit(solution)/shard_map/rpe,rkqe->rkpq/dot_general | solution.py:68
  139.7 1.6 copy.136
  141.3 2.4 pad_maximum_fusion.1
  143.7 4.4 copy.137
  148.1 5.0 %all-to-all-start = ((bf16[1024,4,288]{0,2,1:T(8,128)(2,1)}), bf16[1024,4,288]{0,2,1:T(8,128)(2,1)}, u32[]{:S(2)}, u32[]{:S(2)}) async-start(bf16[1024,4,288]{0,2,1:T(8,128)(2,1)} %bitcast.164), calls=%async_computation | async-start | bytes 4718592 | tf_op jit(solution)/shard_map/all_to_all | solution.py:92
  153.9 3.2 constant_dynamic-slice_fusion
  157.1 3.1 copy.196
  160.2 1.6 constant_dynamic-slice_fusion.1
  161.8 40.9 %all-to-all-done = bf16[1024,4,288]{0,2,1:T(8,128)(2,1)} async-done(((bf16[1024,4,288]{0,2,1:T(8,128)(2,1)}), bf16[1024,4,288]{0,2,1:T(8,128)(2,1)}, u32[]{:S(2)}, u32[]{:S(2)}) %all-to-all-start) | async-done | bytes 2359328 | tf_op jit(solution)/shard_map/all_to_all | solution.py:92
  202.7 2.2 slice_bitcast_fusion.3
  205.0 0.9 copy.145
  206.0 1.0 copy.143
  207.1 0.9 copy.141
  208.1 0.9 copy.138
  209.0 3.3 gather_fusion.4
  212.3 3.3 gather_fusion.3
  215.6 3.3 gather_fusion.2
  219.0 3.4 gather_fusion.1
  222.3 9.9 %all-gather.9.cloned.1.call-done = bf16[3145728]{0:T(1024)(128)(2,1)} async-done(((bf16[786432]{0:T(1024)(128)(2,1)}), bf16[3145728]{0:T(1024)(128)(2,1)}) %all-gather.9.cloned.1.call-update) | async-done | bytes 6291472 | tf_op jit(solution)/shard_map/all_gather | solution.py:87
  232.2 7.7 %reshape.151 = bf16[4,786432]{1,0:T(4,128)(2,1)} reshape(bf16[3145728]{0:T(1024)(128)(2,1)} %all-gather.9.cloned.1.call-done) | data formatting | bytes 12582912 | tf_op jit(solution)/shard_map/all_gather | solution.py:87
  239.9 28.8 %slice_reduce_fusion.3 = (bf16[524288]{0:T(1024)(128)(2,1)S(1)}, bf16[524288]{0:T(1024)(128)(2,1)S(1)}, bf16[524288]{0:T(1024)(128)(2,1)S(1)}, bf16[524288]{0:T(1024)(128)(2,1)S(1)}) fusion(bf16[4,786432]{1,0:T(4,128)(2,1)} %reshape.151), kind=kLoop, calls=%fused_computation.39 | loop fusion | bytes 8388608 | tf_op jit(solution)/shard_map/slice | solution.py:105
  268.8 4.6 slice.79
  274.3 6.1 %fusion.3 = f32[8,128,288,1]{1,0,3,2:T(8,128)S(1)} fusion(f32[8,4,128,288]{2,3,1,0:T(8,128)S(1)} %fusion.76, s32[8,4]{0,1:T(4,128)S(1)} %copy.157), kind=kOutput, calls=%fused_computation.8 | convolution fusion | flops 113246464 | bytes 5898368 | tf_op jit(solution)/shard_map/rkt,rkqe->tqe/dot_general | solution.py:118
  280.4 1.4 copy.218
  282.8 6.1 %fusion.5 = f32[8,128,288,1]{1,0,3,2:T(8,128)S(1)} fusion(f32[8,4,128,288]{2,3,1,0:T(8,128)S(1)} %fusion.75, s32[8,4]{0,1:T(4,128)S(1)} %copy.154), kind=kOutput, calls=%fused_computation.10 | convolution fusion | flops 113246464 | bytes 5898368 | tf_op jit(solution)/shard_map/rkt,rkqe->tqe/dot_general | solution.py:118
  288.9 1.3 copy.219
  291.5 6.1 %fusion.7 = f32[8,128,288,1]{1,0,3,2:T(8,128)S(1)} fusion(f32[8,4,128,288]{2,3,1,0:T(8,128)S(1)} %fusion.74, s32[8,4]{0,1:T(4,128)S(1)} %copy.151), kind=kOutput, calls=%fused_computation.12 | convolution fusion | flops 113246464 | bytes 5898368 | tf_op jit(solution)/shard_map/rkt,rkqe->tqe/dot_general | solution.py:118
  297.6 1.2 copy.220
  298.8 4.5 collective-permute-start.2
  304.2 6.1 %fusion.9 = f32[8,128,288,1]{1,0,3,2:T(8,128)S(1)} fusion(f32[8,4,128,288]{2,3,1,0:T(8,128)S(1)} %fusion.73, s32[8,4]{0,1:T(4,128)S(1)} %copy.147), kind=kOutput, calls=%fused_computation.14 | convolution fusion | flops 113246464 | bytes 5898368 | tf_op jit(solution)/shard_map/rkt,rkqe->tqe/dot_general | solution.py:118
  310.3 1.2 copy.221
  311.6 7.6 %collective-permute-start.1 = (f32[1024,288]{0,1:T(8,128)}, f32[1024,288]{0,1:T(8,128)}, u32[]{:S(2)}, u32[]{:S(2)}) collective-permute-start(f32[1024,288]{0,1:T(8,128)} %bitcast.154), channel_id=1, source_target_pairs={{0,248},{4,252},{8,0},{12,4},{16,8},{20,12},{24,16},{28,20},{32,24... | collective-permute-start | bytes 3538952 | tf_op jit(solution)/shard_map/ppermute | solution.py:14
  319.2 4.8 reshape.99
  324.0 3.2 fusion.12
  327.2 1.1 fusion.14
  329.2 1.1 fusion.16
  331.2 1.1 fusion.18
  332.8 4.8 multiply_reduce_fusion.2
  337.5 21.6 %collective-permute-done.4 = f32[1024,288]{0,1:T(8,128)} collective-permute-done((f32[1024,288]{0,1:T(8,128)}, f32[1024,288]{0,1:T(8,128)}, u32[]{:S(2)}, u32[]{:S(2)}) %collective-permute-start.4) | collective-permute-done | bytes 1179680 | tf_op jit(solution)/shard_map/ppermute | solution.py:14
  359.2 25.0 %collective-permute-done.2 = f32[1024,288]{0,1:T(8,128)} collective-permute-done((f32[1024,288]{0,1:T(8,128)}, f32[1024,288]{0,1:T(8,128)}, u32[]{:S(2)}, u32[]{:S(2)}) %collective-permute-start.2) | collective-permute-done | bytes 1179680 | tf_op jit(solution)/shard_map/ppermute | solution.py:14
  384.1 4.4 multiply_reduce_fusion.3
  388.5 6.1 %all-reduce = (f32[1024]{0:T(1024)S(1)}, f32[1024]{0:T(1024)S(1)}) all-reduce(f32[1024]{0:T(1024)S(1)} %get-tuple-element.35, f32[1024]{0:T(1024)S(1)} %get-tuple-element.37), channel_id=1, replica_groups=mesh['yh'=2,'z'=8,'x'=4,'mp'=4] {'mp'}, use_global_device_ids=true, to_apply=%region_5.7 | all-reduce | flops 2048 | bytes 16384 | tf_op jit(solution)/shard_map/psum | solution.py:122
  394.6 2.7 convolution_bitcast_fusion
  397.5 3.6 convolution_bitcast_fusion.1
  401.1 1.7 pad_maximum_fusion
  402.8 3.5 copy.161
  406.3 4.5 reshape.110
  410.8 3.8 copy.162
  414.6 40.0 %all_to_all.20 = f32[2,8,4,18,576]{4,1,3,0,2:T(8,128)} all-to-all(f32[2,8,4,18,576]{4,1,3,0,2:T(8,128)S(1)} %copy.162), channel_id=1, replica_groups=mesh['yh'=2,'z'=8,'x'=4,'mp'=4] {'x'}, dimensions={2} | all-to-all | bytes 5308416 | tf_op jit(solution)/shard_map/all_to_all | solution.py:24
  454.6 2.1 reduce_sum.67
  457.1 23.8 %all_to_all.21 = f32[2,8,1,18,576]{4,0,3,2,1:T(2,128)S(1)} all-to-all(f32[2,8,1,18,576]{4,0,3,2,1:T(2,128)S(1)} %copy.163), channel_id=1, replica_groups=mesh['yh'=2,'z'=8,'x'=4,'mp'=4] {'z'}, dimensions={1} | all-to-all | bytes 1327104 | tf_op jit(solution)/shard_map/all_to_all | solution.py:24
  481.3 8.5 %all_to_all.22 = f32[2,1,1,18,576]{4,2,3,1,0:T(1,128)S(1)} all-to-all(f32[2,1,1,18,576]{4,2,3,1,0:T(1,128)S(1)} %copy.164), channel_id=1, replica_groups=mesh['yh'=2,'z'=8,'x'=4,'mp'=4] {'yh'}, dimensions={0} | all-to-all | bytes 165888 | tf_op jit(solution)/shard_map/all_to_all | solution.py:24
  (80 shorter events, 11.9 us)
Async XLA Ops:
  7.2 41.4 %copy-start = (bf16[1024,1152]{1,0:T(8,128)(2,1)S(1)}, bf16[1024,1152]{1,0:T(8,128)(2,1)}, u32[]{:S(2)}) copy-start(bf16[1024,1152]{1,0:T(8,128)(2,1)} %param.11) | copy-start | bytes 7077892
  7.2 41.4 %all-gather.7.cloned.1.call-start = ((), (), s32[]{:S(2)}) async-start(), calls=%async_computation.5 | async-start | bytes 3317760 | tf_op jit(solution)/shard_map/all_gather | solution.py:51
  7.9 103.7 %all-gather.5.cloned.1.call-start = ((), (), s32[]{:S(2)}) async-start(), calls=%async_computation.4 | async-start | bytes 3317760 | tf_op jit(solution)/shard_map/all_gather | solution.py:51
  8.7 223.5 %all-gather.9.cloned.1.call-start = ((), (), s32[]{:S(2)}) async-start(), calls=%async_computation.6 | async-start | bytes 7864320 | tf_op jit(solution)/shard_map/all_gather | solution.py:87
  54.0 2.8 copy-start.4
  56.8 67.5 %collective-permute-start = (bf16[1024,1152]{1,0:T(8,128)(2,1)}, bf16[1024,1152]{1,0:T(8,128)(2,1)}, u32[]{:S(2)}, u32[]{:S(2)}) collective-permute-start(bf16[1024,1152]{1,0:T(8,128)(2,1)} %multiply_convert_fusion), channel_id=1, source_target_pairs={{248,0},{5,1},{254,2},{11,3},{252,4},{9,5},{2,6},{15,7},{0,8},{13,... | collective-permute-start | bytes 7077896 | tf_op jit(solution)/shard_map/ppermute | solution.py:60
  117.7 2.1 copy-start.3
  119.8 3.6 copy-start.6
  148.1 54.6 %all-to-all-start = ((bf16[1024,4,288]{0,2,1:T(8,128)(2,1)}), bf16[1024,4,288]{0,2,1:T(8,128)(2,1)}, u32[]{:S(2)}, u32[]{:S(2)}) async-start(bf16[1024,4,288]{0,2,1:T(8,128)(2,1)} %bitcast.164), calls=%async_computation | async-start | bytes 4718592 | tf_op jit(solution)/shard_map/all_to_all | solution.py:92
  268.8 5.5 %copy-start.13 = (bf16[524288]{0:T(1024)(128)(2,1)}, bf16[524288]{0:T(1024)(128)(2,1)S(1)}, u32[]{:S(2)}) copy-start(bf16[524288]{0:T(1024)(128)(2,1)S(1)} %get-tuple-element.4) | copy-start | bytes 3145732
  268.8 13.2 %copy-start.11 = (bf16[524288]{0:T(1024)(128)(2,1)}, bf16[524288]{0:T(1024)(128)(2,1)S(1)}, u32[]{:S(2)}) copy-start(bf16[524288]{0:T(1024)(128)(2,1)S(1)} %get-tuple-element.5) | copy-start | bytes 3145732
  268.8 21.9 %copy-start.9 = (bf16[524288]{0:T(1024)(128)(2,1)}, bf16[524288]{0:T(1024)(128)(2,1)S(1)}, u32[]{:S(2)}) copy-start(bf16[524288]{0:T(1024)(128)(2,1)S(1)} %get-tuple-element.6) | copy-start | bytes 3145732
  268.8 34.6 %copy-start.7 = (bf16[524288]{0:T(1024)(128)(2,1)}, bf16[524288]{0:T(1024)(128)(2,1)S(1)}, u32[]{:S(2)}) copy-start(bf16[524288]{0:T(1024)(128)(2,1)S(1)} %get-tuple-element.3) | copy-start | bytes 3145732
  281.7 77.4 %collective-permute-start.4 = (f32[1024,288]{0,1:T(8,128)}, f32[1024,288]{0,1:T(8,128)}, u32[]{:S(2)}, u32[]{:S(2)}) collective-permute-start(f32[1024,288]{0,1:T(8,128)} %bitcast.151), channel_id=1, source_target_pairs={{0,8},{4,12},{8,16},{12,20},{16,24},{20,28},{24,32},{28,36},{32,40... | collective-permute-start | bytes 3538952 | tf_op jit(solution)/shard_map/ppermute | solution.py:14
  290.2 69.0 %collective-permute-start.3 = (f32[1024,288]{0,1:T(8,128)}, f32[1024,288]{0,1:T(8,128)}, u32[]{:S(2)}, u32[]{:S(2)}) collective-permute-start(f32[1024,288]{0,1:T(8,128)} %bitcast.152), channel_id=1, source_target_pairs={{0,4},{4,8},{8,12},{12,16},{16,20},{20,24},{24,28},{28,32},{32,36}... | collective-permute-start | bytes 3538952 | tf_op jit(solution)/shard_map/ppermute | solution.py:14
  298.8 85.3 %collective-permute-start.2 = (f32[1024,288]{0,1:T(8,128)}, f32[1024,288]{0,1:T(8,128)}, u32[]{:S(2)}, u32[]{:S(2)}) collective-permute-start(f32[1024,288]{0,1:T(8,128)} %bitcast.153), channel_id=1, source_target_pairs={{0,252},{4,0},{8,4},{12,8},{16,12},{20,16},{24,20},{28,24},{32,28}... | collective-permute-start | bytes 3538952 | tf_op jit(solution)/shard_map/ppermute | solution.py:14
  311.6 72.5 %collective-permute-start.1 = (f32[1024,288]{0,1:T(8,128)}, f32[1024,288]{0,1:T(8,128)}, u32[]{:S(2)}, u32[]{:S(2)}) collective-permute-start(f32[1024,288]{0,1:T(8,128)} %bitcast.154), channel_id=1, source_target_pairs={{0,248},{4,252},{8,0},{12,4},{16,8},{20,12},{24,16},{28,20},{32,24... | collective-permute-start | bytes 3538952 | tf_op jit(solution)/shard_map/ppermute | solution.py:14
  324.0 3.2 copy-start.12
  324.0 3.2 copy-start.16
  327.2 1.2 copy-start.10
  327.2 2.0 copy-start.15
  329.2 1.2 copy-start.8
  329.2 2.0 copy-start.14
  331.2 1.6 copy-start.1
  332.8 51.3 %copy-start.2 = (f32[1024,288]{0,1:T(8,128)S(1)}, f32[1024,288]{0,1:T(8,128)}, u32[]{:S(2)}) copy-start(f32[1024,288]{0,1:T(8,128)} %copy.196) | copy-start | bytes 3538948
  394.6 2.8 copy-start.5
  394.6 2.8 copy-start.17
Sparse Core Ops, SparseCore 0:
  9.8 38.7 all-gather.6
  50.4 61.1 all-gather.4
  143.8 88.3 all-gather.8
